TPU v7x, 32 devices: a whole 2x2x4 slice. The times are simulated.
32 devices in a mesh: blk: 4 (over y, core), grp: 8 (over z, x).
Axes of the slice: x: 2, y: 2, z: 4, core: 2. Of those that a mesh axis runs over, the one named last changes fastest.
Arguments:
- features: bfloat16 [4096, 256], P(('blk', 'grp')), may hold values from -6 to 6
- weights: bfloat16 [2, 256, 256], replicated, may hold values from -0.375 to 0.375
- biases: float32 [2, 256], replicated, may hold values from -0.6 to 0.6
- adjacency: bfloat16 [4, 8, 6, 256, 256], P('blk', 'grp'), as said below
- tile_row: int32 [4, 8, 6], P('blk', 'grp'), may hold values from 0 to 1
- tile_column: int32 [4, 8, 6], P('blk', 'grp'), may hold values from 0 to 3
- tile_count: int32 [4, 8], P('blk', 'grp'), may hold values from 1 to 6, as said below
Outputs:
- result: bfloat16 [4096, 256], P(('blk', 'grp'))
Inputs may be any that keep to these rules, and one draw needn't show every extreme that they name: tile_count is at least 1 and at most 6; some device has exactly 6 live slots. `adjacency`: edge weights are zero or positive.
All inputs are finite; a program needn't handle non-finite values.
Results may differ from a plain program's by a relative error of at most 0.0046.
Values may be sent and summed in bfloat16 or wider, within the bound.
No kernel may reach another device: no remote copies, remote signals or barrier semaphores. Data moves between devices by JAX's collectives and lax.ppermute only.
A program may use at most 64 MiB of HBM per device.

v0:
```python
import jax
import jax.numpy as jnp
from jax import lax
from jax.sharding import PartitionSpec as P

LAYERS = 2


def aggregate(adjacency, cols_here, placing, column_rows, row_tiles):
    tile_size = adjacency.shape[1]
    width = column_rows.shape[1]
    blocks = column_rows.reshape(-1, tile_size, width)[cols_here]
    product = jnp.einsum("tij,tjf->tif", adjacency, blocks, preferred_element_type=jnp.float32)
    placed = jnp.einsum("rt,tif->rif", placing, product, precision=lax.Precision.HIGHEST)
    return placed.reshape(row_tiles * tile_size, width)


def on_device(features, weights, biases, adjacency, tile_row, tile_column, tile_count):
    adjacency = adjacency[0, 0]
    rows_here = tile_row[0, 0]
    cols_here = tile_column[0, 0]
    count_here = tile_count[0, 0]
    blk_size = lax.axis_size("blk")
    node_dev = features.shape[0]
    tile_size = adjacency.shape[1]
    slots = adjacency.shape[0]
    width = features.shape[1]
    row_tiles = blk_size * node_dev // tile_size
    live = lax.iota(jnp.int32, slots) < count_here
    placing = (
        (rows_here[None, :] == lax.iota(jnp.int32, row_tiles)[:, None]) & live[None, :]
    ).astype(jnp.float32)
    row_sums = jnp.sum(adjacency, axis=2, dtype=jnp.float32)
    degree_part = jnp.dot(placing, row_sums, precision=lax.Precision.HIGHEST).reshape(
        blk_size, node_dev
    )
    degree = lax.psum_scatter(degree_part, "blk", scatter_dimension=0, tiled=True)[0]
    scale = lax.rsqrt(1.0 + degree)[:, None]
    hidden = features
    result = None
    for layer_index in range(LAYERS):
        mixed = jnp.dot(hidden, weights[layer_index], preferred_element_type=jnp.float32)
        scaled = (mixed * scale).astype(jnp.bfloat16)
        column_rows = lax.all_gather(scaled, "grp", axis=0, tiled=True)
        partial_value = aggregate(adjacency, cols_here, placing, column_rows, row_tiles)
        partial_value = partial_value.reshape(blk_size, node_dev, width)
        summed = lax.psum_scatter(partial_value, "blk", scatter_dimension=0, tiled=True)[0]
        pre = (summed + scaled.astype(jnp.float32)) * scale + biases[layer_index][None, :]
        if layer_index < LAYERS - 1:
            hidden = jnp.maximum(pre, 0.0).astype(jnp.bfloat16)
        else:
            result = pre.astype(jnp.bfloat16)
    return result


def solution(mesh):
    placed = (
        P(("blk", "grp"), None),
        P(),
        P(),
        P("blk", "grp", None, None, None),
        P("blk", "grp", None),
        P("blk", "grp", None),
        P("blk", "grp"),
    )
    return jax.shard_map(
        on_device, mesh=mesh, in_specs=placed, out_specs=P(("blk", "grp"), None), check_vma=False
    )
```

profile of v0, /device:TPU:0, one launch (start us, length us, event | category | flops | bytes accessed | tf_op | source)
XLA Modules:
  0.0 150.4 jit_solution(8604493189462942408)
XLA Ops:
  6.5 0.0 copy-start
  6.5 0.0 reduce-scatter.3.cloned.1.call-start
  7.3 1.4 convert_reduce_fusion
  8.7 0.8 fusion.31
  9.5 8.4 %all-reduce = f32[4,128]{1,0:T(4,128)S(1)} all-reduce(f32[4,128]{1,0:T(4,128)S(1)} %reshape.51), channel_id=2, replica_groups=mesh['blk'=4,'grp'=8] {'blk'}, use_global_device_ids=true, to_apply=%region_1.0.clone | all-reduce | flops 512 | bytes 4096
  17.9 1.2 dynamic-slice
  19.1 0.7 fusion.29
  19.8 1.1 fusion.4
  20.8 31.9 %all_gather.6 = bf16[1024,256]{1,0:T(8,128)(2,1)S(1)} all-gather(bf16[128,256]{1,0:T(8,128)(2,1)S(1)} %fusion.4), channel_id=1, replica_groups=mesh['blk'=4,'grp'=8] {'grp'}, dimensions={0}, use_global_device_ids=true | all-gather | bytes 589824 | tf_op jit(solution)/shard_map/all_gather | solution.py:44
  52.7 0.7 fusion.27
  53.4 0.6 gather_fusion
  54.0 1.6 %fusion.8 = f32[6,256,256]{2,1,0:T(8,128)} fusion(bf16[6,256,256]{2,1,0:T(8,128)(2,1)S(1)} %gather_fusion, bf16[1,1,6,256,256]{4,3,2,1,0:T(8,128)(2,1)S(1)} %copy-done.1), kind=kOutput, calls=%fused_computation.13 | convolution fusion | flops 201326592 | bytes 3145728 | tf_op jit(solution)/shard_map/tij,tjf->tif/dot_general | solution.py:13
  55.6 2.1 %copy.12 = f32[6,256,256]{1,0,2:T(8,128)S(1)} copy(f32[6,256,256]{2,1,0:T(8,128)} %fusion.8) | data formatting | bytes 3145728 | tf_op jit(solution)/shard_map/tij,tjf->tif/dot_general | solution.py:13
  57.7 0.0 copy-done.3
  57.7 0.0 copy-start.4
  57.7 0.0 copy-start.2
  57.7 1.1 fusion.2
  58.8 0.8 copy.10
  59.6 0.0 reduce-scatter.3.cloned.1.call-update
  59.7 0.0 reduce-scatter.5.cloned.1.call-start
  59.7 0.0 copy-done.4
  59.7 21.6 %reduce-scatter.3.cloned.1.call-done = f32[1,128,256]{2,1,0:T(8,128)} async-done(((f32[4,128,256]{2,1,0:T(8,128)}), f32[1,128,256]{2,1,0:T(8,128)}) %reduce-scatter.3.cloned.1.call-update) | async-done | bytes 131088 | tf_op jit(solution)/shard_map/reduce_scatter | solution.py:47
  81.4 1.1 fusion.5
  82.5 31.3 %all_gather.7 = bf16[1024,256]{1,0:T(8,128)(2,1)S(1)} all-gather(bf16[128,256]{1,0:T(8,128)(2,1)S(1)} %fusion.5), channel_id=1, replica_groups=mesh['blk'=4,'grp'=8] {'grp'}, dimensions={0}, use_global_device_ids=true | all-gather | bytes 589824 | tf_op jit(solution)/shard_map/all_gather | solution.py:44
  113.8 0.6 gather_fusion.1
  114.4 1.6 %fusion.6 = f32[6,256,256]{2,1,0:T(8,128)} fusion(bf16[6,256,256]{2,1,0:T(8,128)(2,1)S(1)} %gather_fusion.1, bf16[1,1,6,256,256]{4,3,2,1,0:T(8,128)(2,1)S(1)} %copy-done.1), kind=kOutput, calls=%fused_computation.11 | convolution fusion | flops 201326592 | bytes 3145728 | tf_op jit(solution)/shard_map/tij,tjf->tif/dot_general | solution.py:13
  116.0 2.1 %copy.13 = f32[6,256,256]{1,0,2:T(8,128)S(1)} copy(f32[6,256,256]{2,1,0:T(8,128)} %fusion.6) | data formatting | bytes 3145728 | tf_op jit(solution)/shard_map/tij,tjf->tif/dot_general | solution.py:13
  118.1 1.1 fusion
  119.2 0.8 copy.11
  120.0 0.0 reduce-scatter.5.cloned.1.call-update
  120.0 21.9 %reduce-scatter.5.cloned.1.call-done = f32[1,128,256]{2,1,0:T(8,128)} async-done(((f32[4,128,256]{2,1,0:T(8,128)}), f32[1,128,256]{2,1,0:T(8,128)}) %reduce-scatter.5.cloned.1.call-update) | async-done | bytes 131088 | tf_op jit(solution)/shard_map/reduce_scatter | solution.py:47
  141.9 1.6 %fusion.12 = bf16[128,256]{1,0:T(8,128)(2,1)} fusion(f32[1,128,256]{2,1,0:T(8,128)} %reduce-scatter.5.cloned.1.call-done, bf16[128,256]{1,0:T(8,128)(2,1)S(1)} %fusion.5, f32[256]{0:T(256)S(1)} %bitcast.69, f32[128]{0:T(128)S(1)} %fusion.29), kind=kLoop, calls=%fused_computation.18 | loop fusion | flops 163840 | bytes 263680 | tf_op jit(solution)/shard_map/convert_element_type | solution.py:52
  (9 shorter events, 0.0 us)
Async XLA Ops:
  6.5 13.2 %copy-start = (bf16[128,256]{1,0:T(8,128)(2,1)S(1)}, bf16[128,256]{1,0:T(8,128)(2,1)}, u32[]{:S(2)}) copy-start(bf16[128,256]{1,0:T(8,128)(2,1)} %param.7) | copy-start | bytes 196612
  6.5 47.4 %copy-start.1 = (bf16[1,1,6,256,256]{4,3,2,1,0:T(8,128)(2,1)S(1)}, bf16[1,1,6,256,256]{4,3,2,1,0:T(8,128)(2,1)}, u32[]{:S(2)}) copy-start(bf16[1,1,6,256,256]{4,3,2,1,0:T(8,128)(2,1)} %param.10) | copy-start | bytes 2359300
  6.5 74.8 %reduce-scatter.3.cloned.1.call-start = ((), (), s32[]{:S(2)}) async-start(), calls=%async_computation.2 | async-start | bytes 655360 | tf_op jit(solution)/shard_map/reduce_scatter | solution.py:47
  55.6 2.1 %copy-start.3 = (s32[1,1,6]{2,1,0:T(1,128)S(1)}, s32[1,1,6]{2,1,0:T(1,128)}, u32[]{:S(2)}) copy-start(s32[1,1,6]{2,1,0:T(1,128)} %param.11) | copy-start | bytes 76
  57.7 2.0 %copy-start.4 = (f32[2,256]{1,0:T(2,128)S(1)}, f32[2,256]{1,0:T(2,128)}, u32[]{:S(2)}) copy-start(f32[2,256]{1,0:T(2,128)} %param.9) | copy-start | bytes 6148
  57.7 23.6 %copy-start.2 = (bf16[2,256,256]{2,1,0:T(8,128)(2,1)S(1)}, bf16[2,256,256]{2,1,0:T(8,128)(2,1)}, u32[]{:S(2)}) copy-start(bf16[2,256,256]{2,1,0:T(8,128)(2,1)} %param.8) | copy-start | bytes 786436
  59.7 82.3 %reduce-scatter.5.cloned.1.call-start = ((), (), s32[]{:S(2)}) async-start(), calls=%async_computation.3 | async-start | bytes 655360 | tf_op jit(solution)/shard_map/reduce_scatter | solution.py:47
Sparse Core Ops, SparseCore 0:
  59.8 21.5 reduce-scatter.2
  120.1 21.7 reduce-scatter.4
where the time goes:
time: 151 us; the launch traced here: 150 us
  blocking collectives  71.6 us (47%)
  waiting for transfers between devices  43.6 us (29%)
  between operations  14.3 us (9%)
  local copies, waits for them, and re-layouts  8.33 us (6%)
  matrix products  8.28 us (5%)
  other arithmetic  4.35 us (3%)
    all_gather x2, blocking collectives, on_device(): column_rows = lax.all_gather(scaled, 'grp', axis=0, tiled=True)  63.2 us
    reduce_scatter x2, waiting for transfers between devices, on_device(): lax.psum_scatter(partial_value, 'blk', scatter_dimension=0, tiled=True)[0]  43.5 us
    unnamed x1, blocking collectives  8.36 us
    dot_general x2, local copies, waits for them, and re-layouts, aggregate(): jnp.einsum('tij,tjf->tif', adjacency, blocks, preferred_element_type=jnp....  4.21 us
    dot_general x2, matrix products, aggregate(): jnp.einsum('tij,tjf->tif', adjacency, blocks, preferred_element_type=jnp....  3.17 us
  transfers between devices with their start and end apart: 2, of which 2 were waited for; matrix products, arithmetic and copies ran while one was open for 0% of the time, Pallas kernels for 0%

commit v1 on v0

--- a/solution.py
+++ b/solution.py
@@ -4,6 +4,12 @@
 from jax.sharding import PartitionSpec as P
 
 LAYERS = 2
+
+
+def joined_along(blocks, dim):
+    blocks = jnp.moveaxis(blocks, 0, dim)
+    dims = blocks.shape
+    return blocks.reshape(*dims[:dim], dims[dim] * dims[dim + 1], *dims[dim + 2 :])
 
 
 def aggregate(adjacency, cols_here, placing, column_rows, row_tiles):
@@ -41,7 +47,19 @@
     for layer_index in range(LAYERS):
         mixed = jnp.dot(hidden, weights[layer_index], preferred_element_type=jnp.float32)
         scaled = (mixed * scale).astype(jnp.bfloat16)
-        column_rows = lax.all_gather(scaled, "grp", axis=0, tiled=True)
+        count = lax.axis_size("grp")
+        pairs = [(i, (i + 1) % count) for i in range(count)]
+        back = [(b, a) for a, b in pairs]
+        lower, upper = ([], [])
+        for step in range(count - 1):
+            if step % 2 == 0:
+                lower.append(lax.ppermute(lower[-1] if lower else scaled, "grp", pairs))
+            else:
+                upper.append(lax.ppermute(upper[-1] if upper else scaled, "grp", back))
+        pieces = jnp.stack([*lower[::-1], scaled, *upper])
+        shift = lax.axis_index("grp") - len(lower)
+        pieces = pieces[(jnp.arange(count) - shift) % count]
+        column_rows = joined_along(pieces, 0)
         partial_value = aggregate(adjacency, cols_here, placing, column_rows, row_tiles)
         partial_value = partial_value.reshape(blk_size, node_dev, width)
         summed = lax.psum_scatter(partial_value, "blk", scatter_dimension=0, tiled=True)[0]

time: 151 us -> 145 us (0.960)
  blocking collectives: 71.6 us -> 8.36 us
  starting transfers between devices: 0.04 us -> 30.1 us
  waiting for transfers between devices: 43.6 us -> 69.7 us
    all_gather x2 -> x0, blocking collectives: 63.2 us -> none  [on_device(): column_rows = lax.all_gather(scaled, 'grp', axis=0, tiled=True)]
    ppermute x0 -> x14, starting transfers between devices: none -> 30 us  [the longest x6 26.9 us: on_device(): upper.append(lax.ppermute(upper[-1] if upper else scaled, 'grp', back))]
    ppermute x0 -> x14, waiting for transfers between devices: none -> 25.3 us  [the longest x8 25.3 us: on_device(): lower.append(lax.ppermute(lower[-1] if lower else scaled, 'grp', pairs))]
  transfers between devices with their start and end apart: 2 -> 16, of which waited for: 2 -> 10; matrix products, arithmetic and copies ran while one was open for 0% -> 1% of each run, Pallas kernels for 0% -> 0%
where the time goes in v1:
time: 145 us
  waiting for transfers between devices  69.7 us (48%)
  starting transfers between devices  30.1 us (21%)
  between operations  14.4 us (10%)
  local copies, waits for them, and re-layouts  9.61 us (7%)
  matrix products  8.38 us (6%)
  blocking collectives  8.36 us (6%)
  other arithmetic  4.37 us (3%)
    reduce_scatter x2, waiting for transfers between devices, on_device(): lax.psum_scatter(partial_value, 'blk', scatter_dimension=0, tiled=True)[0]  44.3 us
    ppermute x6, starting transfers between devices, on_device(): upper.append(lax.ppermute(upper[-1] if upper else scaled, 'grp', back))  26.9 us
    ppermute x8, waiting for transfers between devices, on_device(): lower.append(lax.ppermute(lower[-1] if lower else scaled, 'grp', pairs))  25.3 us
    unnamed x1, blocking collectives  8.36 us
    dot_general x2, local copies, waits for them, and re-layouts, aggregate(): jnp.einsum('tij,tjf->tif', adjacency, blocks, preferred_element_type=jnp....  4.21 us
    dot_general x2, matrix products, aggregate(): jnp.einsum('tij,tjf->tif', adjacency, blocks, preferred_element_type=jnp....  3.19 us
    ppermute x8, starting transfers between devices, on_device(): lower.append(lax.ppermute(lower[-1] if lower else scaled, 'grp', pairs))  3.09 us
  transfers between devices with their start and end apart: 16, of which 10 were waited for; matrix products, arithmetic and copies ran while one was open for 1% of the time, Pallas kernels for 0%

profile of v1, /device:TPU:0, one launch (start us, length us, event | category | flops | bytes accessed | tf_op | source)
XLA Modules:
  0.0 144.8 jit_solution(653108213674877496)
XLA Ops:
  7.2 1.4 convert_reduce_fusion
  8.7 0.8 fusion.33
  9.5 8.4 %all-reduce = f32[4,128]{1,0:T(4,128)S(1)} all-reduce(f32[4,128]{1,0:T(4,128)S(1)} %reshape.94), channel_id=2, replica_groups=mesh['blk'=4,'grp'=8] {'blk'}, use_global_device_ids=true, to_apply=%region_1.0.clone | all-reduce | flops 512 | bytes 4096
  17.9 1.2 dynamic-slice
  19.8 1.1 fusion.4
  20.9 1.5 %collective-permute-start = (bf16[128,256]{1,0:T(8,128)(2,1)S(1)}, bf16[128,256]{1,0:T(8,128)(2,1)S(1)}, u32[]{:S(2)}, u32[]{:S(2)}) collective-permute-start(bf16[128,256]{1,0:T(8,128)(2,1)S(1)} %fusion.4), channel_id=1, source_target_pairs={{0,1},{1,2},{2,3},{3,4},{4,5},{5,6},{6,7},{7,0},{8,9},{9,10},{10,1... | collective-permute-start | bytes 196616 | tf_op jit(solution)/shard_map/ppermute | solution.py:56
  22.4 3.2 %collective-permute-start.4 = (bf16[128,256]{1,0:T(8,128)(2,1)S(1)}, bf16[128,256]{1,0:T(8,128)(2,1)S(1)}, u32[]{:S(2)}, u32[]{:S(2)}) collective-permute-start(bf16[128,256]{1,0:T(8,128)(2,1)S(1)} %fusion.4), channel_id=1, source_target_pairs={{1,0},{2,1},{3,2},{4,3},{5,4},{6,5},{7,6},{0,7},{9,8},{10,9},{11,1... | collective-permute-start | bytes 196616 | tf_op jit(solution)/shard_map/ppermute | solution.py:58
  26.3 1.6 %collective-permute-done = bf16[128,256]{1,0:T(8,128)(2,1)S(1)} collective-permute-done((bf16[128,256]{1,0:T(8,128)(2,1)S(1)}, bf16[128,256]{1,0:T(8,128)(2,1)S(1)}, u32[]{:S(2)}, u32[]{:S(2)}) %collective-permute-start) | collective-permute-done | bytes 65568 | tf_op jit(solution)/shard_map/ppermute | solution.py:56
  27.9 7.1 %collective-permute-done.1 = bf16[128,256]{1,0:T(8,128)(2,1)S(1)} collective-permute-done((bf16[128,256]{1,0:T(8,128)(2,1)S(1)}, bf16[128,256]{1,0:T(8,128)(2,1)S(1)}, u32[]{:S(2)}, u32[]{:S(2)}) %collective-permute-start.1) | collective-permute-done | bytes 65568 | tf_op jit(solution)/shard_map/ppermute | solution.py:56
  35.0 4.8 %collective-permute-start.5 = (bf16[128,256]{1,0:T(8,128)(2,1)S(1)}, bf16[128,256]{1,0:T(8,128)(2,1)S(1)}, u32[]{:S(2)}, u32[]{:S(2)}) collective-permute-start(bf16[128,256]{1,0:T(8,128)(2,1)S(1)} %collective-permute-done.4), channel_id=1, source_target_pairs={{1,0},{2,1},{3,2},{4,3},{5,4},{6,5},{7,6},{0,7},{9,8},{10,9},{11,1... | collective-permute-start | bytes 196616 | tf_op jit(solution)/shard_map/ppermute | solution.py:58
  39.7 2.2 %collective-permute-done.2 = bf16[128,256]{1,0:T(8,128)(2,1)S(1)} collective-permute-done((bf16[128,256]{1,0:T(8,128)(2,1)S(1)}, bf16[128,256]{1,0:T(8,128)(2,1)S(1)}, u32[]{:S(2)}, u32[]{:S(2)}) %collective-permute-start.2) | collective-permute-done | bytes 65568 | tf_op jit(solution)/shard_map/ppermute | solution.py:56
  41.9 4.8 %collective-permute-start.6 = (bf16[128,256]{1,0:T(8,128)(2,1)S(1)}, bf16[128,256]{1,0:T(8,128)(2,1)S(1)}, u32[]{:S(2)}, u32[]{:S(2)}) collective-permute-start(bf16[128,256]{1,0:T(8,128)(2,1)S(1)} %collective-permute-done.5), channel_id=1, source_target_pairs={{1,0},{2,1},{3,2},{4,3},{5,4},{6,5},{7,6},{0,7},{9,8},{10,9},{11,1... | collective-permute-start | bytes 196616 | tf_op jit(solution)/shard_map/ppermute | solution.py:58
  46.7 2.2 %collective-permute-done.3 = bf16[128,256]{1,0:T(8,128)(2,1)S(1)} collective-permute-done((bf16[128,256]{1,0:T(8,128)(2,1)S(1)}, bf16[128,256]{1,0:T(8,128)(2,1)S(1)}, u32[]{:S(2)}, u32[]{:S(2)}) %collective-permute-start.3) | collective-permute-done | bytes 65568 | tf_op jit(solution)/shard_map/ppermute | solution.py:56
  50.2 1.6 %fusion.8 = f32[6,256,256]{2,1,0:T(8,128)} fusion(bf16[6,256,256]{2,1,0:T(8,128)(2,1)S(1)} %gather_fusion.1, bf16[1,1,6,256,256]{4,3,2,1,0:T(8,128)(2,1)S(1)} %copy-done.1), kind=kOutput, calls=%fused_computation.15 | convolution fusion | flops 201326592 | bytes 3145728 | tf_op jit(solution)/shard_map/tij,tjf->tif/dot_general | solution.py:19
  51.8 2.1 %copy.12 = f32[6,256,256]{1,0,2:T(8,128)S(1)} copy(f32[6,256,256]{2,1,0:T(8,128)} %fusion.8) | data formatting | bytes 3145728 | tf_op jit(solution)/shard_map/tij,tjf->tif/dot_general | solution.py:19
  54.0 1.1 fusion.2
  56.0 22.2 %reduce-scatter.3.cloned.1.call-done = f32[1,128,256]{2,1,0:T(8,128)} async-done(((f32[4,128,256]{2,1,0:T(8,128)}), f32[1,128,256]{2,1,0:T(8,128)}) %reduce-scatter.3.cloned.1.call-update) | async-done | bytes 131088 | tf_op jit(solution)/shard_map/reduce_scatter | solution.py:65
  78.1 1.1 fusion.5
  79.3 1.5 %collective-permute-start.7 = (bf16[128,256]{1,0:T(8,128)(2,1)S(1)}, bf16[128,256]{1,0:T(8,128)(2,1)S(1)}, u32[]{:S(2)}, u32[]{:S(2)}) collective-permute-start(bf16[128,256]{1,0:T(8,128)(2,1)S(1)} %fusion.5), channel_id=1, source_target_pairs={{0,1},{1,2},{2,3},{3,4},{4,5},{5,6},{6,7},{7,0},{8,9},{9,10},{10,1... | collective-permute-start | bytes 196616 | tf_op jit(solution)/shard_map/ppermute | solution.py:56
  80.8 5.5 %collective-permute-done.7 = bf16[128,256]{1,0:T(8,128)(2,1)S(1)} collective-permute-done((bf16[128,256]{1,0:T(8,128)(2,1)S(1)}, bf16[128,256]{1,0:T(8,128)(2,1)S(1)}, u32[]{:S(2)}, u32[]{:S(2)}) %collective-permute-start.7) | collective-permute-done | bytes 65568 | tf_op jit(solution)/shard_map/ppermute | solution.py:56
  86.3 4.7 %collective-permute-start.11 = (bf16[128,256]{1,0:T(8,128)(2,1)S(1)}, bf16[128,256]{1,0:T(8,128)(2,1)S(1)}, u32[]{:S(2)}, u32[]{:S(2)}) collective-permute-start(bf16[128,256]{1,0:T(8,128)(2,1)S(1)} %fusion.5), channel_id=1, source_target_pairs={{1,0},{2,1},{3,2},{4,3},{5,4},{6,5},{7,6},{0,7},{9,8},{10,9},{11,1... | collective-permute-start | bytes 196616 | tf_op jit(solution)/shard_map/ppermute | solution.py:58
  91.0 2.2 %collective-permute-done.8 = bf16[128,256]{1,0:T(8,128)(2,1)S(1)} collective-permute-done((bf16[128,256]{1,0:T(8,128)(2,1)S(1)}, bf16[128,256]{1,0:T(8,128)(2,1)S(1)}, u32[]{:S(2)}, u32[]{:S(2)}) %collective-permute-start.8) | collective-permute-done | bytes 65568 | tf_op jit(solution)/shard_map/ppermute | solution.py:56
  93.2 4.7 %collective-permute-start.12 = (bf16[128,256]{1,0:T(8,128)(2,1)S(1)}, bf16[128,256]{1,0:T(8,128)(2,1)S(1)}, u32[]{:S(2)}, u32[]{:S(2)}) collective-permute-start(bf16[128,256]{1,0:T(8,128)(2,1)S(1)} %collective-permute-done.11), channel_id=1, source_target_pairs={{1,0},{2,1},{3,2},{4,3},{5,4},{6,5},{7,6},{0,7},{9,8},{10,9},{11,1... | collective-permute-start | bytes 196616 | tf_op jit(solution)/shard_map/ppermute | solution.py:58
  98.0 2.3 %collective-permute-done.9 = bf16[128,256]{1,0:T(8,128)(2,1)S(1)} collective-permute-done((bf16[128,256]{1,0:T(8,128)(2,1)S(1)}, bf16[128,256]{1,0:T(8,128)(2,1)S(1)}, u32[]{:S(2)}, u32[]{:S(2)}) %collective-permute-start.9) | collective-permute-done | bytes 65568 | tf_op jit(solution)/shard_map/ppermute | solution.py:56
  100.3 4.7 %collective-permute-start.13 = (bf16[128,256]{1,0:T(8,128)(2,1)S(1)}, bf16[128,256]{1,0:T(8,128)(2,1)S(1)}, u32[]{:S(2)}, u32[]{:S(2)}) collective-permute-start(bf16[128,256]{1,0:T(8,128)(2,1)S(1)} %collective-permute-done.12), channel_id=1, source_target_pairs={{1,0},{2,1},{3,2},{4,3},{5,4},{6,5},{7,6},{0,7},{9,8},{10,9},{11,1... | collective-permute-start | bytes 196616 | tf_op jit(solution)/shard_map/ppermute | solution.py:58
  105.0 2.2 %collective-permute-done.10 = bf16[128,256]{1,0:T(8,128)(2,1)S(1)} collective-permute-done((bf16[128,256]{1,0:T(8,128)(2,1)S(1)}, bf16[128,256]{1,0:T(8,128)(2,1)S(1)}, u32[]{:S(2)}, u32[]{:S(2)}) %collective-permute-start.10) | collective-permute-done | bytes 65568 | tf_op jit(solution)/shard_map/ppermute | solution.py:56
  108.6 1.6 %fusion.6 = f32[6,256,256]{2,1,0:T(8,128)} fusion(bf16[6,256,256]{2,1,0:T(8,128)(2,1)S(1)} %gather_fusion.3, bf16[1,1,6,256,256]{4,3,2,1,0:T(8,128)(2,1)S(1)} %copy-done.1), kind=kOutput, calls=%fused_computation.13 | convolution fusion | flops 201326592 | bytes 3145728 | tf_op jit(solution)/shard_map/tij,tjf->tif/dot_general | solution.py:19
  110.2 2.1 %copy.13 = f32[6,256,256]{1,0,2:T(8,128)S(1)} copy(f32[6,256,256]{2,1,0:T(8,128)} %fusion.6) | data formatting | bytes 3145728 | tf_op jit(solution)/shard_map/tij,tjf->tif/dot_general | solution.py:19
  112.3 1.1 fusion
  113.4 0.8 copy.11
  114.2 22.2 %reduce-scatter.5.cloned.1.call-done = f32[1,128,256]{2,1,0:T(8,128)} async-done(((f32[4,128,256]{2,1,0:T(8,128)}), f32[1,128,256]{2,1,0:T(8,128)}) %reduce-scatter.5.cloned.1.call-update) | async-done | bytes 131088 | tf_op jit(solution)/shard_map/reduce_scatter | solution.py:65
  136.4 1.6 %fusion.12 = bf16[128,256]{1,0:T(8,128)(2,1)} fusion(f32[1,128,256]{2,1,0:T(8,128)} %reduce-scatter.5.cloned.1.call-done, bf16[128,256]{1,0:T(8,128)(2,1)S(1)} %fusion.5, f32[256]{0:T(256)S(1)} %bitcast.103, f32[128]{0:T(128)S(1)} %fusion.31), kind=kLoop, calls=%fused_computation.20 | loop fusion | flops 163840 | bytes 263680 | tf_op jit(solution)/shard_map/convert_element_type | solution.py:70
  (55 shorter events, 4.8 us)
Async XLA Ops:
  6.5 13.3 %copy-start = (bf16[128,256]{1,0:T(8,128)(2,1)S(1)}, bf16[128,256]{1,0:T(8,128)(2,1)}, u32[]{:S(2)}) copy-start(bf16[128,256]{1,0:T(8,128)(2,1)} %param.7) | copy-start | bytes 196612
  6.5 71.6 %reduce-scatter.3.cloned.1.call-start = ((), (), s32[]{:S(2)}) async-start(), calls=%async_computation.2 | async-start | bytes 655360 | tf_op jit(solution)/shard_map/reduce_scatter | solution.py:65
  8.7 41.5 %copy-start.1 = (bf16[1,1,6,256,256]{4,3,2,1,0:T(8,128)(2,1)S(1)}, bf16[1,1,6,256,256]{4,3,2,1,0:T(8,128)(2,1)}, u32[]{:S(2)}) copy-start(bf16[1,1,6,256,256]{4,3,2,1,0:T(8,128)(2,1)} %param.10) | copy-start | bytes 2359300
  20.9 7.0 %collective-permute-start = (bf16[128,256]{1,0:T(8,128)(2,1)S(1)}, bf16[128,256]{1,0:T(8,128)(2,1)S(1)}, u32[]{:S(2)}, u32[]{:S(2)}) collective-permute-start(bf16[128,256]{1,0:T(8,128)(2,1)S(1)} %fusion.4), channel_id=1, source_target_pairs={{0,1},{1,2},{2,3},{3,4},{4,5},{5,6},{6,7},{7,0},{8,9},{9,10},{10,1... | collective-permute-start | bytes 196616 | tf_op jit(solution)/shard_map/ppermute | solution.py:56
  22.4 12.6 %collective-permute-start.4 = (bf16[128,256]{1,0:T(8,128)(2,1)S(1)}, bf16[128,256]{1,0:T(8,128)(2,1)S(1)}, u32[]{:S(2)}, u32[]{:S(2)}) collective-permute-start(bf16[128,256]{1,0:T(8,128)(2,1)S(1)} %fusion.4), channel_id=1, source_target_pairs={{1,0},{2,1},{3,2},{4,3},{5,4},{6,5},{7,6},{0,7},{9,8},{10,9},{11,1... | collective-permute-start | bytes 196616 | tf_op jit(solution)/shard_map/ppermute | solution.py:58
  27.9 7.1 %collective-permute-start.1 = (bf16[128,256]{1,0:T(8,128)(2,1)S(1)}, bf16[128,256]{1,0:T(8,128)(2,1)S(1)}, u32[]{:S(2)}, u32[]{:S(2)}) collective-permute-start(bf16[128,256]{1,0:T(8,128)(2,1)S(1)} %collective-permute-done), channel_id=1, source_target_pairs={{0,1},{1,2},{2,3},{3,4},{4,5},{5,6},{6,7},{7,0},{8,9},{9,10},{10,1... | collective-permute-start | bytes 196616 | tf_op jit(solution)/shard_map/ppermute | solution.py:56
  35.0 7.0 %collective-permute-start.2 = (bf16[128,256]{1,0:T(8,128)(2,1)S(1)}, bf16[128,256]{1,0:T(8,128)(2,1)S(1)}, u32[]{:S(2)}, u32[]{:S(2)}) collective-permute-start(bf16[128,256]{1,0:T(8,128)(2,1)S(1)} %collective-permute-done.1), channel_id=1, source_target_pairs={{0,1},{1,2},{2,3},{3,4},{4,5},{5,6},{6,7},{7,0},{8,9},{9,10},{10,1... | collective-permute-start | bytes 196616 | tf_op jit(solution)/shard_map/ppermute | solution.py:56
  35.0 7.0 %collective-permute-start.5 = (bf16[128,256]{1,0:T(8,128)(2,1)S(1)}, bf16[128,256]{1,0:T(8,128)(2,1)S(1)}, u32[]{:S(2)}, u32[]{:S(2)}) collective-permute-start(bf16[128,256]{1,0:T(8,128)(2,1)S(1)} %collective-permute-done.4), channel_id=1, source_target_pairs={{1,0},{2,1},{3,2},{4,3},{5,4},{6,5},{7,6},{0,7},{9,8},{10,9},{11,1... | collective-permute-start | bytes 196616 | tf_op jit(solution)/shard_map/ppermute | solution.py:58
  41.9 7.0 %collective-permute-start.3 = (bf16[128,256]{1,0:T(8,128)(2,1)S(1)}, bf16[128,256]{1,0:T(8,128)(2,1)S(1)}, u32[]{:S(2)}, u32[]{:S(2)}) collective-permute-start(bf16[128,256]{1,0:T(8,128)(2,1)S(1)} %collective-permute-done.2), channel_id=1, source_target_pairs={{0,1},{1,2},{2,3},{3,4},{4,5},{5,6},{6,7},{7,0},{8,9},{9,10},{10,1... | collective-permute-start | bytes 196616 | tf_op jit(solution)/shard_map/ppermute | solution.py:56
  41.9 7.0 %collective-permute-start.6 = (bf16[128,256]{1,0:T(8,128)(2,1)S(1)}, bf16[128,256]{1,0:T(8,128)(2,1)S(1)}, u32[]{:S(2)}, u32[]{:S(2)}) collective-permute-start(bf16[128,256]{1,0:T(8,128)(2,1)S(1)} %collective-permute-done.5), channel_id=1, source_target_pairs={{1,0},{2,1},{3,2},{4,3},{5,4},{6,5},{7,6},{0,7},{9,8},{10,9},{11,1... | collective-permute-start | bytes 196616 | tf_op jit(solution)/shard_map/ppermute | solution.py:58
  51.8 2.1 %copy-start.3 = (s32[1,1,6]{2,1,0:T(1,128)S(1)}, s32[1,1,6]{2,1,0:T(1,128)}, u32[]{:S(2)}) copy-start(s32[1,1,6]{2,1,0:T(1,128)} %param.11) | copy-start | bytes 76
  53.9 2.0 %copy-start.4 = (f32[2,256]{1,0:T(2,128)S(1)}, f32[2,256]{1,0:T(2,128)}, u32[]{:S(2)}) copy-start(f32[2,256]{1,0:T(2,128)} %param.9) | copy-start | bytes 6148
  53.9 24.2 %copy-start.2 = (bf16[2,256,256]{2,1,0:T(8,128)(2,1)S(1)}, bf16[2,256,256]{2,1,0:T(8,128)(2,1)}, u32[]{:S(2)}) copy-start(bf16[2,256,256]{2,1,0:T(8,128)(2,1)} %param.8) | copy-start | bytes 786436
  55.9 80.5 %reduce-scatter.5.cloned.1.call-start = ((), (), s32[]{:S(2)}) async-start(), calls=%async_computation.3 | async-start | bytes 655360 | tf_op jit(solution)/shard_map/reduce_scatter | solution.py:65
  79.3 7.0 %collective-permute-start.7 = (bf16[128,256]{1,0:T(8,128)(2,1)S(1)}, bf16[128,256]{1,0:T(8,128)(2,1)S(1)}, u32[]{:S(2)}, u32[]{:S(2)}) collective-permute-start(bf16[128,256]{1,0:T(8,128)(2,1)S(1)} %fusion.5), channel_id=1, source_target_pairs={{0,1},{1,2},{2,3},{3,4},{4,5},{5,6},{6,7},{7,0},{8,9},{9,10},{10,1... | collective-permute-start | bytes 196616 | tf_op jit(solution)/shard_map/ppermute | solution.py:56
  86.3 7.0 %collective-permute-start.8 = (bf16[128,256]{1,0:T(8,128)(2,1)S(1)}, bf16[128,256]{1,0:T(8,128)(2,1)S(1)}, u32[]{:S(2)}, u32[]{:S(2)}) collective-permute-start(bf16[128,256]{1,0:T(8,128)(2,1)S(1)} %collective-permute-done.7), channel_id=1, source_target_pairs={{0,1},{1,2},{2,3},{3,4},{4,5},{5,6},{6,7},{7,0},{8,9},{9,10},{10,1... | collective-permute-start | bytes 196616 | tf_op jit(solution)/shard_map/ppermute | solution.py:56
  86.3 7.0 %collective-permute-start.11 = (bf16[128,256]{1,0:T(8,128)(2,1)S(1)}, bf16[128,256]{1,0:T(8,128)(2,1)S(1)}, u32[]{:S(2)}, u32[]{:S(2)}) collective-permute-start(bf16[128,256]{1,0:T(8,128)(2,1)S(1)} %fusion.5), channel_id=1, source_target_pairs={{1,0},{2,1},{3,2},{4,3},{5,4},{6,5},{7,6},{0,7},{9,8},{10,9},{11,1... | collective-permute-start | bytes 196616 | tf_op jit(solution)/shard_map/ppermute | solution.py:58
  93.2 7.1 %collective-permute-start.9 = (bf16[128,256]{1,0:T(8,128)(2,1)S(1)}, bf16[128,256]{1,0:T(8,128)(2,1)S(1)}, u32[]{:S(2)}, u32[]{:S(2)}) collective-permute-start(bf16[128,256]{1,0:T(8,128)(2,1)S(1)} %collective-permute-done.8), channel_id=1, source_target_pairs={{0,1},{1,2},{2,3},{3,4},{4,5},{5,6},{6,7},{7,0},{8,9},{9,10},{10,1... | collective-permute-start | bytes 196616 | tf_op jit(solution)/shard_map/ppermute | solution.py:56
  93.2 7.1 %collective-permute-start.12 = (bf16[128,256]{1,0:T(8,128)(2,1)S(1)}, bf16[128,256]{1,0:T(8,128)(2,1)S(1)}, u32[]{:S(2)}, u32[]{:S(2)}) collective-permute-start(bf16[128,256]{1,0:T(8,128)(2,1)S(1)} %collective-permute-done.11), channel_id=1, source_target_pairs={{1,0},{2,1},{3,2},{4,3},{5,4},{6,5},{7,6},{0,7},{9,8},{10,9},{11,1... | collective-permute-start | bytes 196616 | tf_op jit(solution)/shard_map/ppermute | solution.py:58
  100.3 7.0 %collective-permute-start.10 = (bf16[128,256]{1,0:T(8,128)(2,1)S(1)}, bf16[128,256]{1,0:T(8,128)(2,1)S(1)}, u32[]{:S(2)}, u32[]{:S(2)}) collective-permute-start(bf16[128,256]{1,0:T(8,128)(2,1)S(1)} %collective-permute-done.9), channel_id=1, source_target_pairs={{0,1},{1,2},{2,3},{3,4},{4,5},{5,6},{6,7},{7,0},{8,9},{9,10},{10,1... | collective-permute-start | bytes 196616 | tf_op jit(solution)/shard_map/ppermute | solution.py:56
  100.3 7.0 %collective-permute-start.13 = (bf16[128,256]{1,0:T(8,128)(2,1)S(1)}, bf16[128,256]{1,0:T(8,128)(2,1)S(1)}, u32[]{:S(2)}, u32[]{:S(2)}) collective-permute-start(bf16[128,256]{1,0:T(8,128)(2,1)S(1)} %collective-permute-done.12), channel_id=1, source_target_pairs={{1,0},{2,1},{3,2},{4,3},{5,4},{6,5},{7,6},{0,7},{9,8},{10,9},{11,1... | collective-permute-start | bytes 196616 | tf_op jit(solution)/shard_map/ppermute | solution.py:58
Sparse Core Ops, SparseCore 0:
  56.0 22.0 reduce-scatter.2
  114.3 22.0 reduce-scatter.4
